TPU v7x, 32 devices: a whole 2x2x4 slice. The times are simulated.
32 devices in a mesh: dp: 8 (over z, core), rot: 4 (over y, x).
Axes of the slice: x: 2, y: 2, z: 4, core: 2. Of those that a mesh axis runs over, the one named last changes fastest.
Arguments:
- vectors: bfloat16 [2048, 4096], P('dp', 'rot'), may hold values from -100 to 100
- rotation: bfloat16 [4096, 4096], P('rot'), may hold values from -0.125 to 0.125
- codes: int32 [2048, 256], P('dp', 'rot'), may hold values from 0 to 255
Outputs:
- codebook: float32 [4096, 256], P('rot')
- new_rotation: bfloat16 [4096, 4096], P('rot', 'dp')
All inputs are finite; a program needn't handle non-finite values.
Results may differ from a plain program's by a relative error of at most 0.007.
Values may be sent and summed in bfloat16 or wider, within the bound.
No kernel may reach another device: no remote copies, remote signals or barrier semaphores. Data moves between devices by JAX's collectives and lax.ppermute only.
A program may use at most 64 MiB of HBM per device.

v0:
```python
import math
import jax
import jax.numpy as jnp
from jax import lax
from jax.sharding import PartitionSpec as P

K = 256
ITERS = 2


def body(vectors, rotation, codes):
    row_count, block_dims = vectors.shape
    width = rotation.shape[1]
    local_spaces = codes.shape[1]
    sub_dims = block_dims // local_spaces
    tile_cols = width // lax.axis_size("dp")
    tile_spaces = tile_cols // sub_dims
    dp_index = lax.axis_index("dp")
    code_ids = jnp.arange(K, dtype=jnp.int32)
    dp_size = lax.axis_size("dp")
    row_codes = lax.all_gather(codes, "rot", axis=1, tiled=True)

    def block_codes(block):
        return lax.dynamic_slice_in_dim(row_codes, block * tile_spaces, tile_spaces, 1).astype(
            jnp.bfloat16
        )

    if dp_size % 2:
        parts = [jnp.concatenate([vectors, block_codes(dp_index)], axis=1)]
        for shift in range(1, dp_size):
            pairs = [(i, (i + shift) % dp_size) for i in range(dp_size)]
            target = (dp_index + shift) % dp_size
            parts.append(
                lax.ppermute(jnp.concatenate([vectors, block_codes(target)], axis=1), "dp", pairs)
            )
        joined = jnp.concatenate(parts, axis=0)
    else:

        def pair_part(block):
            return jnp.concatenate([vectors, block_codes(block), block_codes(block ^ 1)], axis=1)

        parts = [pair_part(dp_index)]
        for shift in range(2, dp_size, 2):
            pairs = [(i, (i + shift) % dp_size) for i in range(dp_size)]
            parts.append(lax.ppermute(pair_part((dp_index + shift) % dp_size), "dp", pairs))
        group = jnp.concatenate(parts, axis=0)
        mine = group[:, : block_dims + tile_spaces]
        for_mate = jnp.concatenate(
            [group[:, :block_dims], group[:, block_dims + tile_spaces :]], axis=1
        )
        mates = [(i, i ^ 1) for i in range(dp_size)]
        joined = jnp.concatenate([mine, lax.ppermute(for_mate, "dp", mates)], axis=0)
    all_vectors = joined[:, :block_dims]
    tile_codes = joined[:, block_dims:].astype(jnp.int32)
    rotated_t = lax.psum_scatter(
        lax.dot_general(
            rotation, vectors, (((0,), (1,)), ((), ())), preferred_element_type=jnp.float32
        ),
        "rot",
        scatter_dimension=0,
        tiled=True,
    ).astype(jnp.bfloat16)
    code_indicator = (codes.T[:, :, None] == code_ids[None, None, :]).astype(jnp.bfloat16)
    grouped_vectors = rotated_t.reshape(local_spaces, sub_dims, row_count)
    shard_code_sums = jnp.einsum(
        "vzo,voc->vzc", grouped_vectors, code_indicator, preferred_element_type=jnp.float32
    )
    local_counts = jnp.sum(code_indicator, axis=1, dtype=jnp.float32)
    total_sums, total_counts = lax.psum((shard_code_sums, local_counts), "dp")
    book = total_sums / jnp.maximum(total_counts, 1.0)[:, None, :]
    codebook = book.reshape(block_dims, K)
    blocks_per_rot = local_spaces // tile_spaces
    offered = lax.dynamic_slice_in_dim(
        book.astype(jnp.bfloat16), dp_index % blocks_per_rot * tile_spaces, tile_spaces, 0
    )
    tile_book = lax.all_gather(offered, "rot", axis=0)[dp_index // blocks_per_rot]
    tile_book, all_vectors, tile_codes = lax.optimization_barrier(
        (tile_book, all_vectors, tile_codes)
    )
    rebuilt_t = jnp.take_along_axis(tile_book, tile_codes.T[:, None, :], axis=2)
    rebuilt_t = rebuilt_t.astype(jnp.bfloat16).reshape(tile_cols, all_vectors.shape[0])
    cross_tile = lax.dot_general(
        all_vectors, rebuilt_t, (((0,), (1,)), ((), ())), preferred_element_type=jnp.float32
    ).astype(jnp.bfloat16)

    def apply_gram(rows_b, gram_b):
        return jnp.dot(
            rows_b,
            lax.all_gather(gram_b, "rot", axis=0, tiled=True),
            preferred_element_type=jnp.float32,
        )

    columns = cross_tile
    new_tile = None
    for iteration in range(ITERS):
        rows_b = lax.all_gather(columns, "dp", axis=1, tiled=True)
        partial = lax.dot_general(
            rows_b, columns, (((0,), (0,)), ((), ())), preferred_element_type=jnp.float32
        ).astype(jnp.bfloat16)
        if iteration == 0:
            gram_part = lax.psum_scatter(partial, "rot", scatter_dimension=0, tiled=True)
        else:
            gram_part = lax.psum(partial, "rot")
        if iteration == 0:
            gram_f = gram_part.astype(jnp.float32)
            total = lax.psum(jnp.sum(gram_f * gram_f), ("dp", "rot"))
            factor = 1.7 / jnp.sqrt(jnp.sqrt(total))
            product = apply_gram(rows_b, gram_part)
            new_tile = factor * (
                1.5 * columns.astype(jnp.float32) - 0.5 * (factor * factor) * product
            )
        else:
            product = jnp.dot(rows_b, gram_part, preferred_element_type=jnp.float32)
            new_tile = 1.5 * columns.astype(jnp.float32) - 0.5 * product
        columns = new_tile.astype(jnp.bfloat16)
    new_rotation = (math.sqrt(width) * new_tile).astype(jnp.bfloat16)
    return (codebook, new_rotation)


def solution(mesh):
    return jax.shard_map(
        body,
        mesh=mesh,
        in_specs=(P("dp", "rot"), P("rot", None), P("dp", "rot")),
        out_specs=(P("rot", None), P("rot", "dp")),
        check_vma=False,
    )
```

profile of v0, /device:TPU:0, one launch (start us, length us, event | category | flops | bytes accessed | tf_op | source)
XLA Modules:
  0.0 1250.6 jit_solution(5058009144251274857)
XLA Ops:
  7.2 7.8 fusion.17
  15.2 0.9 copy-done.6
  16.1 0.2 copy.28
  16.4 11.0 all_gather.20
  27.4 0.1 pad_maximum_fusion.1
  27.5 1.8 collective-permute-start
  29.3 3.0 collective-permute-start.1
  32.3 1.2 collective-permute-start.2
  33.4 3.4 convert_reduce_fusion
  36.9 8.4 collective-permute-done
  45.3 19.9 %collective-permute-done.1 = bf16[256,1088]{0,1:T(8,128)(2,1)S(1)} collective-permute-done((bf16[256,1088]{0,1:T(8,128)(2,1)S(1)}, bf16[256,1088]{0,1:T(8,128)(2,1)S(1)}, u32[]{:S(2)}, u32[]{:S(2)}) %collective-permute-start.1) | collective-permute-done | bytes 557088 | tf_op jit(solution)/shard_map/ppermute | solution.py:45
  65.2 0.8 copy-done.1
  66.0 0.2 copy-done.2
  66.2 2.4 pad_maximum_fusion
  68.7 1.5 slice.23
  70.2 1.0 reduce-scatter.3.cloned.1.call-done
  71.2 1.3 convert_element_type.63
  72.5 5.1 fusion.1
  77.7 4.2 fusion.14
  81.9 64.6 %all-reduce.6.cloned.1.call-done = (f32[64,16,256]{2,1,0:T(8,128)}, f32[64,256]{1,0:T(8,128)}) async-done(((f32[64,16,256]{2,1,0:T(8,128)}, f32[64,256]{1,0:T(8,128)}), (f32[64,16,256]{2,1,0:T(8,128)}, f32[64,256]{1,0:T(8,128)})) %all-reduce.6.cloned.1.call-update) | async-done | bytes 1114128 | tf_op jit(solution)/shard_map/psum | solution.py:69
  146.5 0.8 broadcast_maximum_fusion
  147.3 1.3 broadcast_divide_fusion
  148.7 0.8 dynamic-slice_convert_fusion
  149.6 0.2 slice.22
  149.8 0.9 fusion.16
  150.7 3.4 fusion.8
  154.1 21.1 %all-gather.12.cloned.1.call-done = bf16[128,16,256]{2,1,0:T(8,128)(2,1)} async-done(((bf16[32,16,256]{2,1,0:T(8,128)(2,1)}), bf16[128,16,256]{2,1,0:T(8,128)(2,1)}) %all-gather.12.cloned.1.call-update) | async-done | bytes 1048592 | tf_op jit(solution)/shard_map/all_gather | solution.py:76
  175.2 1.0 constant_dynamic-slice_fusion
  176.2 1.0 copy.33
  177.3 0.1 fusion.15
  177.4 634.4 %gather_fusion = bf16[65536,16]{1,0:T(8,128)(2,1)} fusion(bf16[32,16,256]{1,2,0:T(8,128)(2,1)S(1)} %bitcast.37, s32[65536]{0:T(1024)S(1)} %bitcast.36), kind=kCustom, calls=%fused_computation | custom fusion | bytes 4718592 | tf_op jit(solution)/shard_map/jit(take_along_axis)/gather | solution.py:80
  811.8 12.8 %copy.32 = bf16[32,2048,16]{1,2,0:T(8,128)(2,1)S(1)} copy(bf16[32,2048,16]{2,1,0:T(8,128)(2,1)} %bitcast.38) | data formatting | bytes 4194304 | tf_op jit(solution)/shard_map/jit(take_along_axis)/gather | solution.py:80
  824.6 0.3 broadcast_select_fusion
  825.0 1.8 copy-done
  826.8 3.3 convolution_convert_fusion.2
  830.2 0.2 reduce-scatter.5.cloned.1.call-start
  830.4 82.0 %all-gather.6.cloned.1.call-done = bf16[1024,4096]{1,0:T(8,128)(2,1)} async-done(((bf16[1024,512]{1,0:T(8,128)(2,1)}), bf16[1024,4096]{1,0:T(8,128)(2,1)}) %all-gather.6.cloned.1.call-update) | async-done | bytes 8388624 | tf_op jit(solution)/shard_map/all_gather | solution.py:96
  912.4 10.2 convolution_convert_fusion.1
  922.6 51.2 %reduce-scatter.5.cloned.1.call-done = bf16[1024,512]{1,0:T(8,128)(2,1)} async-done(((bf16[4096,512]{1,0:T(8,128)(2,1)}), bf16[1024,512]{1,0:T(8,128)(2,1)}) %reduce-scatter.5.cloned.1.call-update) | async-done | bytes 1048592 | tf_op jit(solution)/shard_map/reduce_scatter | solution.py:101
  973.9 2.4 multiply_reduce_fusion
  976.3 40.4 %psum.30 = f32[]{:T(128)} all-reduce(f32[]{:T(128)} %multiply_reduce_fusion), channel_id=1, replica_groups=mesh['dp'=8,'rot'=4] {'dp','rot'}, use_global_device_ids=true, to_apply=%region_6.7 | all-reduce | flops 1 | bytes 8 | tf_op jit(solution)/shard_map/psum | solution.py:106
  1017.3 11.5 all-gather.8.cloned.1.call-done
  1028.9 10.1 multiply_convert_fusion.1
  1039.0 0.3 all-reduce.4.cloned.1.call-start
  1039.3 81.9 %all-gather.10.cloned.1.call-done = bf16[1024,4096]{1,0:T(8,128)(2,1)} async-done(((bf16[1024,512]{1,0:T(8,128)(2,1)}), bf16[1024,4096]{1,0:T(8,128)(2,1)}) %all-gather.10.cloned.1.call-update) | async-done | bytes 8388624 | tf_op jit(solution)/shard_map/all_gather | solution.py:96
  1121.2 10.1 convolution_convert_fusion
  1131.3 102.3 %all-reduce.4.cloned.1.call-done = bf16[4096,512]{1,0:T(8,128)(2,1)} async-done(((bf16[4096,512]{1,0:T(8,128)(2,1)}), bf16[4096,512]{1,0:T(8,128)(2,1)}) %all-reduce.4.cloned.1.call-update) | async-done | bytes 4194320 | tf_op jit(solution)/shard_map/psum | solution.py:103
  1233.6 10.1 multiply_convert_fusion
  (32 shorter events, 0.6 us)
Async XLA Ops:
  7.2 64.0 %reduce-scatter.3.cloned.1.call-start = ((), (), s32[]{:S(2)}) async-start(), calls=%async_computation.2 | async-start | bytes 5242880 | tf_op jit(solution)/shard_map/reduce_scatter | solution.py:55
  15.1 1.0 copy-start.6
  15.1 1.3 copy-start.7
  15.1 131.4 %all-reduce.6.cloned.1.call-start = ((), (), s32[]{:S(2)}) async-start(), calls=%async_computation.9 | async-start | bytes 2228224 | tf_op jit(solution)/shard_map/psum | solution.py:69
  27.5 17.8 %collective-permute-start = (bf16[256,1088]{0,1:T(8,128)(2,1)S(1)}, bf16[256,1088]{0,1:T(8,128)(2,1)S(1)}, u32[]{:S(2)}, u32[]{:S(2)}) collective-permute-start(bf16[256,1088]{0,1:T(8,128)(2,1)S(1)} %get-tuple-element.10), channel_id=1, source_target_pairs={{0,8},{4,12},{8,16},{12,20},{16,24},{20,28},{24,0},{28,4},{1,9},{5... | collective-permute-start | bytes 1671176 | tf_op jit(solution)/shard_map/ppermute | solution.py:45
  29.3 35.9 %collective-permute-start.1 = (bf16[256,1088]{0,1:T(8,128)(2,1)S(1)}, bf16[256,1088]{0,1:T(8,128)(2,1)S(1)}, u32[]{:S(2)}, u32[]{:S(2)}) collective-permute-start(bf16[256,1088]{0,1:T(8,128)(2,1)S(1)} %get-tuple-element.11), channel_id=1, source_target_pairs={{0,16},{4,20},{8,24},{12,28},{16,0},{20,4},{24,8},{28,12},{1,17},{... | collective-permute-start | bytes 1671176 | tf_op jit(solution)/shard_map/ppermute | solution.py:45
  32.3 33.0 %collective-permute-start.2 = (bf16[256,1088]{0,1:T(8,128)(2,1)S(1)}, bf16[256,1088]{0,1:T(8,128)(2,1)S(1)}, u32[]{:S(2)}, u32[]{:S(2)}) collective-permute-start(bf16[256,1088]{0,1:T(8,128)(2,1)S(1)} %get-tuple-element.12), channel_id=1, source_target_pairs={{0,24},{4,28},{8,0},{12,4},{16,8},{20,12},{24,16},{28,20},{1,25},{... | collective-permute-start | bytes 1671176 | tf_op jit(solution)/shard_map/ppermute | solution.py:45
  65.2 0.8 copy-start.1
  65.2 1.0 copy-start.2
  77.6 97.6 %all-gather.12.cloned.1.call-start = ((), (), s32[]{:S(2)}) async-start(), calls=%async_computation.8 | async-start | bytes 1310720 | tf_op jit(solution)/shard_map/all_gather | solution.py:76
  81.9 67.9 %collective-permute-start.3 = (bf16[1024,1056]{0,1:T(8,128)(2,1)}, bf16[1024,1056]{0,1:T(8,128)(2,1)}, u32[]{:S(2)}, u32[]{:S(2)}) collective-permute-start(bf16[1024,1056]{0,1:T(8,128)(2,1)} %fusion.14), channel_id=1, source_target_pairs={{0,4},{4,0},{8,12},{12,8},{16,20},{20,16},{24,28},{28,24},{1,5},{5... | collective-permute-start | bytes 6488072 | tf_op jit(solution)/shard_map/ppermute | solution.py:52
  148.7 2.0 copy-start.3
  149.5 762.8 %all-gather.6.cloned.1.call-start = ((), (), s32[]{:S(2)}) async-start(), calls=%async_computation.3 | async-start | bytes 9437184 | tf_op jit(solution)/shard_map/all_gather | solution.py:96
  824.6 2.2 copy-start
  830.2 143.6 %reduce-scatter.5.cloned.1.call-start = ((), (), s32[]{:S(2)}) async-start(), calls=%async_computation.4 | async-start | bytes 5242880 | tf_op jit(solution)/shard_map/reduce_scatter | solution.py:101
  922.5 106.4 %copy-start.4 = (bf16[1024,512]{1,0:T(8,128)(2,1)S(1)}, bf16[1024,512]{1,0:T(8,128)(2,1)}, u32[]{:S(2)}) copy-start(bf16[1024,512]{1,0:T(8,128)(2,1)} %convolution_convert_fusion.2) | copy-start | bytes 3145732
  922.5 106.3 %all-gather.8.cloned.1.call-start = ((), (), s32[]{:S(2)}) async-start(), calls=%async_computation.5 | async-start | bytes 5242880 | tf_op jit(solution)/shard_map/all_gather | solution.py:89
  973.8 147.4 %all-gather.10.cloned.1.call-start = ((), (), s32[]{:S(2)}) async-start(), calls=%async_computation.6 | async-start | bytes 9437184 | tf_op jit(solution)/shard_map/all_gather | solution.py:96
  1039.0 194.6 %all-reduce.4.cloned.1.call-start = ((), (), s32[]{:S(2)}) async-start(), calls=%async_computation.7 | async-start | bytes 8388608 | tf_op jit(solution)/shard_map/psum | solution.py:103
  1131.3 102.3 %copy-start.5 = (bf16[1024,512]{1,0:T(8,128)(2,1)S(1)}, bf16[1024,512]{1,0:T(8,128)(2,1)}, u32[]{:S(2)}) copy-start(bf16[1024,512]{1,0:T(8,128)(2,1)} %multiply_convert_fusion.1) | copy-start | bytes 3145732
Sparse Core Ops, SparseCore 0:
  15.2 55.9 reduce-scatter.2
  77.7 68.7 all-reduce.5
  149.7 25.4 all-gather.11
  830.3 82.0 all-gather.5
  922.7 51.0 reduce-scatter.4
  975.5 53.3 all-gather.7
  1039.1 82.0 all-gather.9
  1131.5 102.0 all-reduce.3
where the time goes:
time: 1250 us
  local copies, waits for them, and re-layouts  656 us (52%)
  waiting for transfers between devices  444 us (36%)
  matrix products  56.8 us (5%)
  blocking collectives  51.4 us (4%)
  other arithmetic  20.8 us (2%)
  between operations  15.1 us (1%)
    gather x2, local copies, waits for them, and re-layouts, body(): rebuilt_t = jnp.take_along_axis(tile_book, tile_codes.T[:, None, :], axis=2)  647 us
    all_gather x2, waiting for transfers between devices, body(): rows_b = lax.all_gather(columns, 'dp', axis=1, tiled=True)  164 us
    psum x1, waiting for transfers between devices, body(): gram_part = lax.psum(partial, 'rot')  102 us
    psum x1, waiting for transfers between devices, body(): total_sums, total_counts = lax.psum((shard_code_sums, local_counts), 'dp')  64.6 us
    reduce_scatter x1, waiting for transfers between devices, body(): lax.psum_scatter(partial, 'rot', scatter_dimension=0, tiled=True)  51.2 us
    psum x1, blocking collectives, body(): total = lax.psum(jnp.sum(gram_f * gram_f), ('dp', 'rot'))  40.4 us
    ppermute x3, waiting for transfers between devices, body(): lax.ppermute(pair_part((dp_index + shift) % dp_size), 'dp', pairs)  28.4 us
  transfers between devices with their start and end apart: 12, of which 10 were waited for; matrix products, arithmetic and copies ran while one was open for 2% of the time, Pallas kernels for 0%

commit v1 on v0

--- a/solution.py
+++ b/solution.py
@@ -93,7 +93,18 @@
     columns = cross_tile
     new_tile = None
     for iteration in range(ITERS):
-        rows_b = lax.all_gather(columns, "dp", axis=1, tiled=True)
+        side_arr = lax.axis_size("dp")
+        res = lax.axis_index("dp")
+        local_part, o_now = (side_arr, res)
+        rows_b, moved = (columns, 1)
+        while moved < local_part:
+            r1 = lax.ppermute(
+                rows_b, "dp", perm=[(hop_no, hop_no ^ moved) for hop_no in range(local_part)]
+            )
+            work_now = jnp.concatenate([rows_b, r1], 1)
+            b_now = jnp.concatenate([r1, rows_b], 1)
+            rows_b = jnp.where(o_now & moved == 0, work_now, b_now)
+            moved = 2 * moved
         partial = lax.dot_general(
             rows_b, columns, (((0,), (0,)), ((), ())), preferred_element_type=jnp.float32
         ).astype(jnp.bfloat16)

time: 1250 us -> 1580 us (1.26)
  waiting for transfers between devices: 444 us -> 741 us
    ppermute x0 -> x6, waiting for transfers between devices: none -> 459 us  [body(): lax.ppermute(rows_b, 'dp', perm=[(hop_no, hop_no ^ moved) for hop_no in r...]
    all_gather x2 -> x0, waiting for transfers between devices: 164 us -> none  [body(): rows_b = lax.all_gather(columns, 'dp', axis=1, tiled=True)]
  transfers between devices with their start and end apart: 12 -> 16, of which waited for: 10 -> 14; matrix products, arithmetic and copies ran while one was open for 2% -> 1% of each run, Pallas kernels for 0% -> 0%
where the time goes in v1:
time: 1580 us
  waiting for transfers between devices  741 us (47%)
  local copies, waits for them, and re-layouts  662 us (42%)
  matrix products  60.3 us (4%)
  blocking collectives  51.6 us (3%)
  other arithmetic  31.6 us (2%)
    gather x2, local copies, waits for them, and re-layouts, body(): rebuilt_t = jnp.take_along_axis(tile_book, tile_codes.T[:, None, :], axis=2)  652 us
    ppermute x6, waiting for transfers between devices, body(): lax.ppermute(rows_b, 'dp', perm=[(hop_no, hop_no ^ moved) for hop_no in r...  459 us
    psum x1, waiting for transfers between devices, body(): gram_part = lax.psum(partial, 'rot')  104 us
    psum x1, waiting for transfers between devices, body(): total_sums, total_counts = lax.psum((shard_code_sums, local_counts), 'dp')  64.6 us
    reduce_scatter x1, waiting for transfers between devices, body(): lax.psum_scatter(partial, 'rot', scatter_dimension=0, tiled=True)  52.7 us
    psum x1, blocking collectives, body(): total = lax.psum(jnp.sum(gram_f * gram_f), ('dp', 'rot'))  40.5 us
  transfers between devices with their start and end apart: 16, of which 14 were waited for; matrix products, arithmetic and copies ran while one was open for 1% of the time, Pallas kernels for 0%

profile of v1, /device:TPU:0, one launch (start us, length us, event | category | flops | bytes accessed | tf_op | source)
XLA Modules:
  0.0 1576.4 jit_solution(1411329849431476164)
XLA Ops:
  7.2 7.9 fusion.21
  16.4 11.0 all_gather.14
  27.5 1.8 collective-permute-start
  29.3 3.0 collective-permute-start.1
  32.3 1.2 collective-permute-start.2
  33.5 3.4 convert_reduce_fusion
  36.9 8.4 collective-permute-done
  45.3 19.9 %collective-permute-done.1 = bf16[256,1088]{0,1:T(8,128)(2,1)S(1)} collective-permute-done((bf16[256,1088]{0,1:T(8,128)(2,1)S(1)}, bf16[256,1088]{0,1:T(8,128)(2,1)S(1)}, u32[]{:S(2)}, u32[]{:S(2)}) %collective-permute-start.1) | collective-permute-done | bytes 557088 | tf_op jit(solution)/shard_map/ppermute | solution.py:45
  66.2 2.4 pad_maximum_fusion
  68.7 1.5 slice.23
  70.2 1.0 reduce-scatter.3.cloned.1.call-done
  71.2 1.3 convert_element_type.63
  72.5 5.1 fusion.1
  77.7 4.2 fusion.14
  81.9 64.6 %all-reduce.6.cloned.1.call-done = (f32[64,16,256]{2,1,0:T(8,128)}, f32[64,256]{1,0:T(8,128)}) async-done(((f32[64,16,256]{2,1,0:T(8,128)}, f32[64,256]{1,0:T(8,128)}), (f32[64,16,256]{2,1,0:T(8,128)}, f32[64,256]{1,0:T(8,128)})) %all-reduce.6.cloned.1.call-update) | async-done | bytes 1114128 | tf_op jit(solution)/shard_map/psum | solution.py:69
  147.4 1.3 broadcast_divide_fusion
  150.9 3.4 fusion.8
  154.3 20.9 %all-gather.6.cloned.1.call-done = bf16[128,16,256]{2,1,0:T(8,128)(2,1)} async-done(((bf16[32,16,256]{2,1,0:T(8,128)(2,1)}), bf16[128,16,256]{2,1,0:T(8,128)(2,1)}) %all-gather.6.cloned.1.call-update) | async-done | bytes 1048592 | tf_op jit(solution)/shard_map/all_gather | solution.py:76
  175.2 1.0 constant_dynamic-slice_fusion
  176.2 1.0 copy.40
  177.5 639.2 %gather_fusion = bf16[65536,16]{1,0:T(8,128)(2,1)} fusion(bf16[32,16,256]{1,2,0:T(8,128)(2,1)S(1)} %bitcast.33, s32[65536]{0:T(1024)S(1)} %bitcast.32), kind=kCustom, calls=%fused_computation | custom fusion | bytes 4718592 | tf_op jit(solution)/shard_map/jit(take_along_axis)/gather | solution.py:80
  816.7 12.8 copy.36
  829.8 1.8 copy-done.1
  831.7 2.4 convolution_convert_fusion.2
  834.1 2.8 collective-permute-done.4
  836.9 2.6 maximum_select_fusion.4
  839.5 1.6 collective-permute-start.5
  841.1 46.3 %collective-permute-done.5 = bf16[1024,1024]{0,1:T(8,128)(2,1)} collective-permute-done((bf16[1024,1024]{0,1:T(8,128)(2,1)S(1)}, bf16[1024,1024]{0,1:T(8,128)(2,1)}, u32[]{:S(2)}, u32[]{:S(2)}) %collective-permute-start.5) | collective-permute-done | bytes 2097184 | tf_op jit(solution)/shard_map/ppermute | solution.py:101
  887.4 4.9 maximum_select_fusion.2
  892.2 2.4 collective-permute-start.6
  894.7 180.4 %collective-permute-done.6 = bf16[1024,2048]{0,1:T(8,128)(2,1)} collective-permute-done((bf16[1024,2048]{0,1:T(8,128)(2,1)}, bf16[1024,2048]{0,1:T(8,128)(2,1)}, u32[]{:S(2)}, u32[]{:S(2)}) %collective-permute-start.6) | collective-permute-done | bytes 4194336 | tf_op jit(solution)/shard_map/ppermute | solution.py:101
  1075.1 11.6 convolution_convert_fusion.1
  1086.7 52.7 %reduce-scatter.5.cloned.1.call-done = bf16[1024,512]{1,0:T(8,128)(2,1)} async-done(((bf16[4096,512]{1,0:T(8,128)(2,1)}), bf16[1024,512]{1,0:T(8,128)(2,1)}) %reduce-scatter.5.cloned.1.call-update) | async-done | bytes 1048592 | tf_op jit(solution)/shard_map/reduce_scatter | solution.py:112
  1139.5 2.4 multiply_reduce_fusion
  1141.8 40.5 %psum.30 = f32[]{:T(128)} all-reduce(f32[]{:T(128)} %multiply_reduce_fusion), channel_id=1, replica_groups=mesh['dp'=8,'rot'=4] {'dp','rot'}, use_global_device_ids=true, to_apply=%region_6.7 | all-reduce | flops 1 | bytes 8 | tf_op jit(solution)/shard_map/psum | solution.py:117
  1183.1 11.4 all-gather.4.cloned.1.call-done
  1194.5 9.8 multiply_convert_fusion.1
  1204.4 2.6 collective-permute-done.7
  1207.1 1.0 maximum_select_fusion.5
  1208.1 1.5 collective-permute-start.8
  1209.6 46.2 %collective-permute-done.8 = bf16[1024,1024]{0,1:T(8,128)(2,1)S(1)} collective-permute-done((bf16[1024,1024]{0,1:T(8,128)(2,1)S(1)}, bf16[1024,1024]{0,1:T(8,128)(2,1)S(1)}, u32[]{:S(2)}, u32[]{:S(2)}) %collective-permute-start.8) | collective-permute-done | bytes 2097184 | tf_op jit(solution)/shard_map/ppermute | solution.py:101
  1255.8 2.3 maximum_select_fusion.3
  1258.2 2.5 collective-permute-start.9
  1260.6 180.2 %collective-permute-done.9 = bf16[1024,2048]{0,1:T(8,128)(2,1)} collective-permute-done((bf16[1024,2048]{0,1:T(8,128)(2,1)S(1)}, bf16[1024,2048]{0,1:T(8,128)(2,1)}, u32[]{:S(2)}, u32[]{:S(2)}) %collective-permute-start.9) | collective-permute-done | bytes 4194336 | tf_op jit(solution)/shard_map/ppermute | solution.py:101
  1440.9 13.7 convolution_convert_fusion
  1454.6 103.7 %all-reduce.4.cloned.1.call-done = bf16[4096,512]{1,0:T(8,128)(2,1)} async-done(((bf16[4096,512]{1,0:T(8,128)(2,1)}), bf16[4096,512]{1,0:T(8,128)(2,1)}) %all-reduce.4.cloned.1.call-update) | async-done | bytes 4194320 | tf_op jit(solution)/shard_map/psum | solution.py:114
  1558.4 9.8 multiply_convert_fusion
  1568.2 1.3 copy.38
  (41 shorter events, 6.1 us)
Async XLA Ops:
  7.2 64.0 %reduce-scatter.3.cloned.1.call-start = ((), (), s32[]{:S(2)}) async-start(), calls=%async_computation.2 | async-start | bytes 5242880 | tf_op jit(solution)/shard_map/reduce_scatter | solution.py:55
  15.1 1.0 copy-start.5
  15.1 1.3 copy-start.6
  15.1 131.4 %all-reduce.6.cloned.1.call-start = ((), (), s32[]{:S(2)}) async-start(), calls=%async_computation.7 | async-start | bytes 2228224 | tf_op jit(solution)/shard_map/psum | solution.py:69
  27.5 17.8 %collective-permute-start = (bf16[256,1088]{0,1:T(8,128)(2,1)S(1)}, bf16[256,1088]{0,1:T(8,128)(2,1)S(1)}, u32[]{:S(2)}, u32[]{:S(2)}) collective-permute-start(bf16[256,1088]{0,1:T(8,128)(2,1)S(1)} %get-tuple-element.16), channel_id=1, source_target_pairs={{0,8},{4,12},{8,16},{12,20},{16,24},{20,28},{24,0},{28,4},{1,9},{5... | collective-permute-start | bytes 1671176 | tf_op jit(solution)/shard_map/ppermute | solution.py:45
  29.3 35.9 %collective-permute-start.1 = (bf16[256,1088]{0,1:T(8,128)(2,1)S(1)}, bf16[256,1088]{0,1:T(8,128)(2,1)S(1)}, u32[]{:S(2)}, u32[]{:S(2)}) collective-permute-start(bf16[256,1088]{0,1:T(8,128)(2,1)S(1)} %get-tuple-element.17), channel_id=1, source_target_pairs={{0,16},{4,20},{8,24},{12,28},{16,0},{20,4},{24,8},{28,12},{1,17},{... | collective-permute-start | bytes 1671176 | tf_op jit(solution)/shard_map/ppermute | solution.py:45
  32.3 33.0 %collective-permute-start.2 = (bf16[256,1088]{0,1:T(8,128)(2,1)S(1)}, bf16[256,1088]{0,1:T(8,128)(2,1)S(1)}, u32[]{:S(2)}, u32[]{:S(2)}) collective-permute-start(bf16[256,1088]{0,1:T(8,128)(2,1)S(1)} %get-tuple-element.18), channel_id=1, source_target_pairs={{0,24},{4,28},{8,0},{12,4},{16,8},{20,12},{24,16},{28,20},{1,25},{... | collective-permute-start | bytes 1671176 | tf_op jit(solution)/shard_map/ppermute | solution.py:45
  65.2 0.8 copy-start.2
  65.2 1.0 copy-start.3
  77.6 97.6 %all-gather.6.cloned.1.call-start = ((), (), s32[]{:S(2)}) async-start(), calls=%async_computation.6 | async-start | bytes 1310720 | tf_op jit(solution)/shard_map/all_gather | solution.py:76
  81.9 68.1 %collective-permute-start.3 = (bf16[1024,1056]{0,1:T(8,128)(2,1)}, bf16[1024,1056]{0,1:T(8,128)(2,1)}, u32[]{:S(2)}, u32[]{:S(2)}) collective-permute-start(bf16[1024,1056]{0,1:T(8,128)(2,1)} %fusion.14), channel_id=1, source_target_pairs={{0,4},{4,0},{8,12},{12,8},{16,20},{20,16},{24,28},{28,24},{1,5},{5... | collective-permute-start | bytes 6488072 | tf_op jit(solution)/shard_map/ppermute | solution.py:52
  148.7 2.2 copy-start.4
  149.6 989.8 %reduce-scatter.5.cloned.1.call-start = ((), (), s32[]{:S(2)}) async-start(), calls=%async_computation.3 | async-start | bytes 5242880 | tf_op jit(solution)/shard_map/reduce_scatter | solution.py:112
  829.5 2.2 copy-start.1
  834.1 2.9 collective-permute-start.4
  839.5 47.8 %collective-permute-start.5 = (bf16[1024,1024]{0,1:T(8,128)(2,1)S(1)}, bf16[1024,1024]{0,1:T(8,128)(2,1)}, u32[]{:S(2)}, u32[]{:S(2)}) collective-permute-start(bf16[1024,1024]{0,1:T(8,128)(2,1)S(1)} %maximum_select_fusion.4), channel_id=1, source_target_pairs={{0,8},{4,12},{8,0},{12,4},{16,24},{20,28},{24,16},{28,20},{1,9},{5... | collective-permute-start | bytes 6291464 | tf_op jit(solution)/shard_map/ppermute | solution.py:101
  892.2 182.9 %collective-permute-start.6 = (bf16[1024,2048]{0,1:T(8,128)(2,1)}, bf16[1024,2048]{0,1:T(8,128)(2,1)}, u32[]{:S(2)}, u32[]{:S(2)}) collective-permute-start(bf16[1024,2048]{0,1:T(8,128)(2,1)} %maximum_select_fusion.2), channel_id=1, source_target_pairs={{0,16},{4,20},{8,24},{12,28},{16,0},{20,4},{24,8},{28,12},{1,17},{... | collective-permute-start | bytes 12582920 | tf_op jit(solution)/shard_map/ppermute | solution.py:101
  1086.7 107.8 %all-gather.4.cloned.1.call-start = ((), (), s32[]{:S(2)}) async-start(), calls=%async_computation.4 | async-start | bytes 5242880 | tf_op jit(solution)/shard_map/all_gather | solution.py:89
  1139.4 419.0 %all-reduce.4.cloned.1.call-start = ((), (), s32[]{:S(2)}) async-start(), calls=%async_computation.5 | async-start | bytes 8388608 | tf_op jit(solution)/shard_map/psum | solution.py:114
  1204.3 2.7 collective-permute-start.7
  1208.1 47.7 %collective-permute-start.8 = (bf16[1024,1024]{0,1:T(8,128)(2,1)S(1)}, bf16[1024,1024]{0,1:T(8,128)(2,1)S(1)}, u32[]{:S(2)}, u32[]{:S(2)}) collective-permute-start(bf16[1024,1024]{0,1:T(8,128)(2,1)S(1)} %maximum_select_fusion.5), channel_id=1, source_target_pairs={{0,8},{4,12},{8,0},{12,4},{16,24},{20,28},{24,16},{28,20},{1,9},{5... | collective-permute-start | bytes 6291464 | tf_op jit(solution)/shard_map/ppermute | solution.py:101
  1258.1 182.7 %copy-start = (bf16[1024,2048]{0,1:T(8,128)(2,1)}, bf16[1024,2048]{0,1:T(8,128)(2,1)S(1)}, u32[]{:S(2)}) copy-start(bf16[1024,2048]{0,1:T(8,128)(2,1)S(1)} %maximum_select_fusion.3) | copy-start | bytes 12582916
  1258.2 182.7 %collective-permute-start.9 = (bf16[1024,2048]{0,1:T(8,128)(2,1)S(1)}, bf16[1024,2048]{0,1:T(8,128)(2,1)}, u32[]{:S(2)}, u32[]{:S(2)}) collective-permute-start(bf16[1024,2048]{0,1:T(8,128)(2,1)S(1)} %maximum_select_fusion.3), channel_id=1, source_target_pairs={{0,16},{4,20},{8,24},{12,28},{16,0},{20,4},{24,8},{28,12},{1,17},{... | collective-permute-start | bytes 12582920 | tf_op jit(solution)/shard_map/ppermute | solution.py:101
Sparse Core Ops, SparseCore 0:
  15.2 55.9 reduce-scatter.2
  77.7 68.7 all-reduce.5
  149.7 25.4 all-gather.5
  1086.8 52.5 reduce-scatter.4
  1141.1 53.3 all-gather.3
  1454.8 103.5 all-reduce.3
